TPU v7x, 256 devices: a whole 4x4x8 slice. The times are simulated.
256 devices in a mesh: hyp: 32 (over y, x, core), head: 8 (over z).
Axes of the slice: x: 4, y: 4, z: 8, core: 2. Of those that a mesh axis runs over, the one named last changes fastest.
Arguments:
- step_embeds: bfloat16 [3, 512, 4096], P(None, 'hyp'), may hold values from -6 to 6
- lang_table: bfloat16 [8, 4096], replicated, may hold values from -3 to 3
- lang_ids: int32 [32, 4], replicated, may hold values from 0 to 7
- self_gain: float32 [4096], replicated, may hold values from 0.1 to 1.9
- self_wq: bfloat16 [4096, 2048], P(None, 'head'), may hold values from -0.09375 to 0.09375
- self_wk: bfloat16 [4096, 2048], P(None, 'head'), may hold values from -0.09375 to 0.09375
- self_wv: bfloat16 [4096, 2048], P(None, 'head'), may hold values from -0.09375 to 0.09375
- self_wo: bfloat16 [2048, 4096], P('head'), may hold values from -0.125 to 0.125
- cross_gain: float32 [4096], replicated, may hold values from 0.1 to 1.9
- cross_wq: bfloat16 [4096, 2048], P(None, 'head'), may hold values from -0.09375 to 0.09375
- cross_wkv: bfloat16 [4096, 4096], P('hyp', 'head'), may hold values from -0.09375 to 0.09375
- encoder_rows: bfloat16 [24576, 4096], P('hyp', 'head'), may hold values from -200 to 200
- doc_lengths: int32 [32], P('hyp'), may hold values from 192 to 768, as said below
- past_keys: bfloat16 [512, 32, 2048], P('hyp', None, 'head'), may hold values from -200 to 200
- past_values: bfloat16 [512, 32, 2048], P('hyp', None, 'head'), may hold values from -6 to 6
- parents: int32 [3, 512], replicated, may hold values from 0 to 3
Outputs:
- cross_context: bfloat16 [3, 512, 2048], P(None, 'hyp', 'head')
- final_keys: bfloat16 [512, 35, 2048], P('hyp', None, 'head')
- final_values: bfloat16 [512, 35, 2048], P('hyp', None, 'head')
Inputs may be any that keep to these rules, and one draw needn't show every extreme that they name: `doc_lengths`: some document has exactly 768 live rows. `parents`: A parent is a beam of the same document and target.
All inputs are finite; a program needn't handle non-finite values.
Results may differ from a plain program's by a relative error of at most 0.03.
Values may be sent and summed in bfloat16 or wider, within the bound.
No kernel may reach another device: no remote copies, remote signals or barrier semaphores. Data moves between devices by JAX's collectives and lax.ppermute only.
A program may use at most 128 MiB of HBM per device.

v0:
```python
import jax
import jax.numpy as jnp
from jax import lax
from jax.sharding import PartitionSpec as P

HEAD = 256
BEAMS = 4
TARGETS = 4
STEPS = 3
EPSILON = 1e-06


def rms_scaled(values_in, gain):
    mean_square = jnp.mean(values_in * values_in, axis=-1, keepdims=True)
    return values_in * lax.rsqrt(mean_square + EPSILON) * gain


def pick_rows(candidates, selector, row_axis):
    shape_list = [1] * candidates[0].ndim
    shape_list[row_axis] = selector.shape[0]
    chosen = candidates[0]
    for position in range(1, len(candidates)):
        chosen = jnp.where((selector == position).reshape(shape_list), candidates[position], chosen)
    return chosen


def beam_copies(block, hyp_count, group_size):
    copies = [block]
    for hop in range(1, BEAMS):
        distance = hop * group_size
        route = [((i - distance) % hyp_count, i) for i in range(hyp_count)]
        copies.append(lax.ppermute(block, "hyp", route))
    return copies


def cross_attend(queries, cross_keys, cross_values, doc_length, scaling):
    scores = (
        jnp.einsum("qd,jd->qj", queries, cross_keys, preferred_element_type=jnp.float32) * scaling
    )
    live_mask = lax.broadcasted_iota(jnp.int32, (1, cross_keys.shape[0]), 1) < doc_length
    scores = jnp.where(live_mask, scores, -jnp.inf)
    highest = jnp.max(scores, axis=1, keepdims=True)
    raw_weights = jnp.exp(scores - highest)
    totals = jnp.sum(raw_weights, axis=1, keepdims=True)
    weights = (raw_weights / totals).astype(jnp.bfloat16)
    output = jnp.einsum("qj,jd->qd", weights, cross_values, preferred_element_type=jnp.float32)
    return output.astype(jnp.bfloat16)


def shards(
    step_embeds,
    lang_table,
    lang_ids,
    self_gain,
    self_wq,
    self_wk,
    self_wv,
    self_wo,
    cross_gain,
    cross_wq,
    cross_wkv,
    encoder_rows,
    doc_lengths,
    past_keys,
    past_values,
    parents,
):
    hyp_count = lax.axis_size("hyp")
    group_size = hyp_count // BEAMS
    my_index = lax.axis_index("hyp")
    my_beam = my_index // group_size
    my_slot = my_index % group_size
    steps = step_embeds.shape[0]
    row_count = step_embeds.shape[1]
    docs_here = row_count // TARGETS
    head_width = self_wq.shape[1]
    doc_count = lang_ids.shape[0]
    past_len = past_keys.shape[1]
    scaling = HEAD ** (-0.5)
    full_weights = lax.all_gather(cross_wkv, "hyp", axis=0, tiled=True)
    full_rows = lax.all_gather(encoder_rows, "head", axis=1, tiled=True)
    cross_kv = jnp.dot(full_rows, full_weights, preferred_element_type=jnp.float32).astype(
        jnp.bfloat16
    )
    cross_kv = cross_kv.reshape(encoder_rows.shape[0], 2, HEAD)
    cross_keys = cross_kv[:, 0, :]
    cross_values = cross_kv[:, 1, :]
    doc_length = doc_lengths[0]
    past_stack = jnp.stack([past_keys, past_values])
    past_all = beam_copies(past_stack, hyp_count, group_size)
    my_langs = lax.dynamic_slice_in_dim(lang_ids, my_slot * docs_here, docs_here, 0).reshape(
        row_count
    )
    one_hot = (
        my_langs[:, None] == lax.broadcasted_iota(jnp.int32, (1, lang_table.shape[0]), 1)
    ).astype(jnp.bfloat16)
    lang_rows = jnp.dot(one_hot, lang_table, preferred_element_type=jnp.float32)
    hidden_in = step_embeds.astype(jnp.float32) + lang_rows[None]
    normed = rms_scaled(hidden_in, self_gain).astype(jnp.bfloat16).reshape(steps * row_count, -1)
    new_query = jnp.dot(normed, self_wq, preferred_element_type=jnp.float32).astype(jnp.bfloat16)
    new_key = jnp.dot(normed, self_wk, preferred_element_type=jnp.float32).astype(jnp.bfloat16)
    new_value = jnp.dot(normed, self_wv, preferred_element_type=jnp.float32).astype(jnp.bfloat16)
    new_query = new_query.reshape(steps, row_count, head_width)
    fresh = jnp.stack([new_key, new_value]).reshape(2, steps, row_count, head_width)
    fresh_all = beam_copies(fresh, hyp_count, group_size)
    parent_view = parents.reshape(steps, BEAMS, doc_count * TARGETS)
    parent_of = lax.dynamic_slice_in_dim(parent_view, my_slot * row_count, row_count, 2)
    own_beam = jnp.full((row_count,), my_beam, jnp.int32)

    def hop_of(beam):
        return (my_beam - beam) % BEAMS

    def climb(step_idx, beam):
        return jnp.take_along_axis(parent_of[step_idx], beam[None, :], axis=0)[0]

    def cache_at(step_idx):
        ancestor = own_beam
        new_parts = [None] * (step_idx + 1)
        new_parts[step_idx] = fresh[:, step_idx]
        for back in range(step_idx, 0, -1):
            ancestor = climb(back, ancestor)
            new_parts[back - 1] = pick_rows(
                [f[:, back - 1] for f in fresh_all], hop_of(ancestor), 1
            )
        ancestor = climb(0, ancestor)
        past_part = pick_rows(past_all, hop_of(ancestor), 1)
        return jnp.concatenate([past_part] + [n[:, :, None, :] for n in new_parts], axis=2)

    contexts = []
    final_cache = None
    for step_idx in range(steps):
        cache = cache_at(step_idx)
        if step_idx == steps - 1:
            final_cache = cache
        query = new_query[step_idx]
        scores = (
            jnp.einsum("rd,rpd->rp", query, cache[0], preferred_element_type=jnp.float32) * scaling
        )
        highest = jnp.max(scores, axis=1, keepdims=True)
        raw_weights = jnp.exp(scores - highest)
        totals = jnp.sum(raw_weights, axis=1, keepdims=True)
        summed = jnp.einsum(
            "rp,rpd->rd",
            raw_weights,
            cache[1].astype(jnp.float32),
            preferred_element_type=jnp.float32,
        )
        contexts.append((summed / totals).astype(jnp.bfloat16))
    self_context = jnp.stack(contexts).reshape(steps * row_count, head_width)
    partial_out = jnp.dot(self_context, self_wo, preferred_element_type=jnp.float32)
    summed_out = lax.psum(partial_out.astype(jnp.bfloat16), "head").astype(jnp.float32)
    residual = hidden_in + summed_out.reshape(hidden_in.shape)
    normed_cross = rms_scaled(residual, cross_gain).astype(jnp.bfloat16)
    cross_query = jnp.dot(
        normed_cross.reshape(steps * row_count, -1), cross_wq, preferred_element_type=jnp.float32
    ).astype(jnp.bfloat16)
    by_doc = cross_query.reshape(steps, docs_here, TARGETS, head_width)
    sent = []
    for shift in range(BEAMS):
        route = [
            (beam * group_size + slot, slot * docs_here + (beam + shift) % BEAMS)
            for beam in range(BEAMS)
            for slot in range(group_size)
        ]
        piece = lax.dynamic_index_in_dim(by_doc, (my_beam + shift) % BEAMS, 1, keepdims=False)
        sent.append(lax.ppermute(piece, "hyp", route))
    doc_queries = jnp.stack(sent).reshape(BEAMS * steps * TARGETS, head_width)
    answer = cross_attend(doc_queries, cross_keys, cross_values, doc_length, scaling)
    answer = answer.reshape(BEAMS, steps, TARGETS, head_width)
    back = []
    for shift in range(BEAMS):
        route = [
            (slot * docs_here + (beam + shift) % BEAMS, beam * group_size + slot)
            for beam in range(BEAMS)
            for slot in range(group_size)
        ]
        back.append(lax.ppermute(answer[shift], "hyp", route))
    back = jnp.stack(back)
    order = (jnp.arange(docs_here, dtype=jnp.int32) - my_beam) % BEAMS
    by_k = jnp.take(back, order, axis=0)
    contexts_out = by_k.transpose(1, 0, 2, 3).reshape(steps, row_count, head_width)
    return (contexts_out, final_cache[0], final_cache[1])


def solution(mesh):
    return jax.shard_map(
        shards,
        mesh=mesh,
        in_specs=(
            P(None, "hyp", None),
            P(),
            P(),
            P(),
            P(None, "head"),
            P(None, "head"),
            P(None, "head"),
            P("head", None),
            P(),
            P(None, "head"),
            P("hyp", "head"),
            P("hyp", "head"),
            P("hyp"),
            P("hyp", None, "head"),
            P("hyp", None, "head"),
            P(),
        ),
        out_specs=(P(None, "hyp", "head"), P("hyp", None, "head"), P("hyp", None, "head")),
        check_vma=False,
    )
```

profile of v0, /device:TPU:17, one launch (start us, length us, event | category | flops | bytes accessed | tf_op | source)
XLA Modules:
  0.0 224.9 jit_solution(5241141596806689058)
XLA Ops:
  8.1 0.9 constant_dynamic-slice_fusion
  9.2 1.1 fusion.42
  10.2 1.3 multiply_reduce_fusion.1
  11.6 1.2 multiply_convert_fusion.1
  12.8 2.1 convolution_convert_fusion.4
  15.6 2.6 %collective-permute-start.4 = (bf16[2,3,16,256]{3,2,0,1:T(8,128)(2,1)S(1)}, bf16[2,3,16,256]{3,2,0,1:T(8,128)(2,1)S(1)}, u32[]{:S(2)}, u32[]{:S(2)}) collective-permute-start(bf16[2,3,16,256]{3,2,0,1:T(8,128)(2,1)S(1)} %pad_maximum_fusion.4), channel_id=1, source_target_pairs={{128,0},{136,8},{144,16},{152,24},{160,32},{168,40},{176,48},{184,... | collective-permute-start | bytes 147464 | tf_op jit(solution)/shard_map/ppermute | solution.py:32
  18.6 0.8 pad_maximum_fusion.2
  19.4 1.5 collective-permute-start
  20.9 1.6 collective-permute-start.1
  25.1 1.2 gather_fusion.5
  27.7 0.7 gather_fusion.3
  28.4 1.2 broadcast_compare_fusion.16
  30.1 1.1 broadcast_compare_fusion.6
  32.0 2.1 convolution_convert_fusion.6
  34.7 11.1 %collective-permute-done.2 = bf16[2,16,32,256]{3,1,2,0:T(8,128)(2,1)S(1)} collective-permute-done((bf16[2,16,32,256]{3,1,2,0:T(8,128)(2,1)}, bf16[2,16,32,256]{3,1,2,0:T(8,128)(2,1)S(1)}, u32[]{:S(2)}, u32[]{:S(2)}) %collective-permute-start.2) | collective-permute-done | bytes 524320 | tf_op jit(solution)/shard_map/ppermute | solution.py:32
  45.8 1.5 select_select_fusion.2
  50.2 1.2 convolution_convert_fusion
  53.4 78.1 %all-reduce.2.cloned.1.call-done = bf16[3,16,4096]{2,1,0:T(8,128)(2,1)} async-done(((bf16[3,16,4096]{2,1,0:T(8,128)(2,1)}), bf16[3,16,4096]{2,1,0:T(8,128)(2,1)}) %all-reduce.2.cloned.1.call-update) | async-done | bytes 393232 | tf_op jit(solution)/shard_map/psum | solution.py:151
  131.6 1.4 multiply_reduce_fusion
  133.0 1.2 multiply_convert_fusion
  134.7 4.6 %collective-permute-start.9 = (bf16[3,4,256]{2,1,0:T(4,128)(2,1)S(1)}, bf16[3,4,256]{2,1,0:T(4,128)(2,1)S(1)}, u32[]{:S(2)}, u32[]{:S(2)}) collective-permute-start(bf16[3,4,256]{2,1,0:T(4,128)(2,1)S(1)} %get-tuple-element.43), channel_id=1, source_target_pairs={{0,24},{8,56},{16,88},{24,120},{32,152},{40,184},{48,216},{56,248}... | collective-permute-start | bytes 18440 | tf_op jit(solution)/shard_map/ppermute | solution.py:166
  139.3 12.5 %collective-permute-start.8 = (bf16[3,4,256]{2,1,0:T(4,128)(2,1)S(1)}, bf16[3,4,256]{2,1,0:T(4,128)(2,1)S(1)}, u32[]{:S(2)}, u32[]{:S(2)}) collective-permute-start(bf16[3,4,256]{2,1,0:T(4,128)(2,1)S(1)} %get-tuple-element.44), channel_id=1, source_target_pairs={{0,16},{8,48},{16,80},{24,112},{32,144},{40,176},{48,208},{56,240}... | collective-permute-start | bytes 18440 | tf_op jit(solution)/shard_map/ppermute | solution.py:166
  151.8 5.5 %collective-permute-start.7 = (bf16[3,4,256]{2,1,0:T(4,128)(2,1)S(1)}, bf16[3,4,256]{2,1,0:T(4,128)(2,1)S(1)}, u32[]{:S(2)}, u32[]{:S(2)}) collective-permute-start(bf16[3,4,256]{2,1,0:T(4,128)(2,1)S(1)} %get-tuple-element.45), channel_id=1, source_target_pairs={{0,8},{8,40},{16,72},{24,104},{32,136},{40,168},{48,200},{56,232},... | collective-permute-start | bytes 18440 | tf_op jit(solution)/shard_map/ppermute | solution.py:166
  157.3 3.3 %collective-permute-start.6 = (bf16[3,4,256]{2,1,0:T(4,128)(2,1)S(1)}, bf16[3,4,256]{2,1,0:T(4,128)(2,1)S(1)}, u32[]{:S(2)}, u32[]{:S(2)}) collective-permute-start(bf16[3,4,256]{2,1,0:T(4,128)(2,1)S(1)} %get-tuple-element.42), channel_id=1, source_target_pairs={{0,0},{8,32},{16,64},{24,96},{32,128},{40,160},{48,192},{56,224},{... | collective-permute-start | bytes 18440 | tf_op jit(solution)/shard_map/ppermute | solution.py:166
  160.6 4.0 %collective-permute-done.6 = bf16[3,4,256]{2,1,0:T(4,128)(2,1)S(1)} collective-permute-done((bf16[3,4,256]{2,1,0:T(4,128)(2,1)S(1)}, bf16[3,4,256]{2,1,0:T(4,128)(2,1)S(1)}, u32[]{:S(2)}, u32[]{:S(2)}) %collective-permute-start.6) | collective-permute-done | bytes 6176 | tf_op jit(solution)/shard_map/ppermute | solution.py:166
  164.7 21.2 %all-gather.3.cloned.1.call-done = bf16[768,4096]{1,0:T(8,128)(2,1)} async-done(((bf16[768,512]{1,0:T(8,128)(2,1)}), bf16[768,4096]{1,0:T(8,128)(2,1)}) %all-gather.3.cloned.1.call-update) | async-done | bytes 6291472 | tf_op jit(solution)/shard_map/all_gather | solution.py:81
  186.0 7.5 %convolution_convert_fusion.1 = bf16[768,512]{0,1:T(8,128)(2,1)S(1)} fusion(bf16[768,4096]{1,0:T(8,128)(2,1)} %all-gather.3.cloned.1.call-done, bf16[4096,512]{1,0:T(8,128)(2,1)} %all-gather.5.cloned.1.call-done), kind=kOutput, calls=%fused_computation.8 | convolution fusion | flops 3221618688 | bytes 11272192 | tf_op jit(solution)/shard_map/dot_general | solution.py:82
  194.3 5.6 %collective-permute-start.13 = (bf16[3,4,256]{2,1,0:T(4,128)(2,1)S(1)}, bf16[3,4,256]{2,1,0:T(4,128)(2,1)S(1)}, u32[]{:S(2)}, u32[]{:S(2)}) collective-permute-start(bf16[3,4,256]{2,1,0:T(4,128)(2,1)S(1)} %squeeze.124), channel_id=1, source_target_pairs={{24,0},{56,8},{88,16},{120,24},{152,32},{184,40},{216,48},{248,56}... | collective-permute-start | bytes 18440 | tf_op jit(solution)/shard_map/ppermute | solution.py:177
  199.9 1.7 collective-permute-start.12
  201.7 5.9 %collective-permute-start.11 = (bf16[3,4,256]{2,1,0:T(4,128)(2,1)S(1)}, bf16[3,4,256]{2,1,0:T(4,128)(2,1)S(1)}, u32[]{:S(2)}, u32[]{:S(2)}) collective-permute-start(bf16[3,4,256]{2,1,0:T(4,128)(2,1)S(1)} %squeeze.122), channel_id=1, source_target_pairs={{8,0},{40,8},{72,16},{104,24},{136,32},{168,40},{200,48},{232,56},... | collective-permute-start | bytes 18440 | tf_op jit(solution)/shard_map/ppermute | solution.py:177
  207.6 2.9 %collective-permute-start.10 = (bf16[3,4,256]{2,1,0:T(4,128)(2,1)S(1)}, bf16[3,4,256]{2,1,0:T(4,128)(2,1)S(1)}, u32[]{:S(2)}, u32[]{:S(2)}) collective-permute-start(bf16[3,4,256]{2,1,0:T(4,128)(2,1)S(1)} %squeeze.121), channel_id=1, source_target_pairs={{0,0},{32,8},{64,16},{96,24},{128,32},{160,40},{192,48},{224,56},{... | collective-permute-start | bytes 18440 | tf_op jit(solution)/shard_map/ppermute | solution.py:177
  210.6 5.6 %collective-permute-done.10 = bf16[3,4,256]{2,1,0:T(4,128)(2,1)S(1)} collective-permute-done((bf16[3,4,256]{2,1,0:T(4,128)(2,1)S(1)}, bf16[3,4,256]{2,1,0:T(4,128)(2,1)S(1)}, u32[]{:S(2)}, u32[]{:S(2)}) %collective-permute-start.10) | collective-permute-done | bytes 6176 | tf_op jit(solution)/shard_map/ppermute | solution.py:177
  (132 shorter events, 13.9 us)
Async XLA Ops:
  8.0 42.2 %copy-start = (bf16[256,4096]{1,0:T(8,128)(2,1)S(1)}, bf16[256,4096]{1,0:T(8,128)(2,1)}, u32[]{:S(2)}) copy-start(bf16[256,4096]{1,0:T(8,128)(2,1)} %param.25) | copy-start | bytes 6291460
  8.0 123.5 %all-reduce.2.cloned.1.call-start = ((), (), s32[]{:S(2)}) async-start(), calls=%async_computation | async-start | bytes 786432 | tf_op jit(solution)/shard_map/psum | solution.py:151
  10.2 4.7 %copy-start.2 = (bf16[4096,256]{1,0:T(8,128)(2,1)S(1)}, bf16[4096,256]{1,0:T(8,128)(2,1)}, u32[]{:S(2)}) copy-start(bf16[4096,256]{1,0:T(8,128)(2,1)} %param.23) | copy-start | bytes 6291460
  12.7 5.5 %copy-start.6 = (bf16[16,32,256]{2,1,0:T(8,128)(2,1)S(1)}, bf16[16,32,256]{2,1,0:T(8,128)(2,1)}, u32[]{:S(2)}) copy-start(bf16[16,32,256]{2,1,0:T(8,128)(2,1)} %param.32) | copy-start | bytes 786436
  12.7 5.5 %copy-start.7 = (bf16[16,32,256]{2,1,0:T(8,128)(2,1)S(1)}, bf16[16,32,256]{2,1,0:T(8,128)(2,1)}, u32[]{:S(2)}) copy-start(bf16[16,32,256]{2,1,0:T(8,128)(2,1)} %param.31) | copy-start | bytes 786436
  14.9 7.5 %copy-start.9 = (s32[3,512]{1,0:T(4,128)S(1)}, s32[3,512]{1,0:T(4,128)}, u32[]{:S(2)}) copy-start(s32[3,512]{1,0:T(4,128)} %param.33) | copy-start | bytes 18436
  15.4 18.8 %collective-permute-start.3 = (bf16[2,3,16,256]{3,2,0,1:T(8,128)(2,1)S(1)}, bf16[2,3,16,256]{3,2,0,1:T(8,128)(2,1)S(1)}, u32[]{:S(2)}, u32[]{:S(2)}) collective-permute-start(bf16[2,3,16,256]{3,2,0,1:T(8,128)(2,1)S(1)} %pad_maximum_fusion.4), channel_id=1, source_target_pairs={{64,0},{72,8},{80,16},{88,24},{96,32},{104,40},{112,48},{120,56},{... | collective-permute-start | bytes 147464 | tf_op jit(solution)/shard_map/ppermute | solution.py:32
  15.6 18.8 %collective-permute-start.4 = (bf16[2,3,16,256]{3,2,0,1:T(8,128)(2,1)S(1)}, bf16[2,3,16,256]{3,2,0,1:T(8,128)(2,1)S(1)}, u32[]{:S(2)}, u32[]{:S(2)}) collective-permute-start(bf16[2,3,16,256]{3,2,0,1:T(8,128)(2,1)S(1)} %pad_maximum_fusion.4), channel_id=1, source_target_pairs={{128,0},{136,8},{144,16},{152,24},{160,32},{168,40},{176,48},{184,... | collective-permute-start | bytes 147464 | tf_op jit(solution)/shard_map/ppermute | solution.py:32
  18.3 16.2 %collective-permute-start.5 = (bf16[2,3,16,256]{3,2,0,1:T(8,128)(2,1)S(1)}, bf16[2,3,16,256]{3,2,0,1:T(8,128)(2,1)S(1)}, u32[]{:S(2)}, u32[]{:S(2)}) collective-permute-start(bf16[2,3,16,256]{3,2,0,1:T(8,128)(2,1)S(1)} %pad_maximum_fusion.4), channel_id=1, source_target_pairs={{192,0},{200,8},{208,16},{216,24},{224,32},{232,40},{240,48},{248,... | collective-permute-start | bytes 147464 | tf_op jit(solution)/shard_map/ppermute | solution.py:32
  19.4 15.3 %collective-permute-start = (bf16[2,16,32,256]{3,1,2,0:T(8,128)(2,1)}, bf16[2,16,32,256]{3,1,2,0:T(8,128)(2,1)}, u32[]{:S(2)}, u32[]{:S(2)}) collective-permute-start(bf16[2,16,32,256]{3,1,2,0:T(8,128)(2,1)} %pad_maximum_fusion.2), channel_id=1, source_target_pairs={{64,0},{72,8},{80,16},{88,24},{96,32},{104,40},{112,48},{120,56},{... | collective-permute-start | bytes 1572872 | tf_op jit(solution)/shard_map/ppermute | solution.py:32
  20.9 13.8 %collective-permute-start.1 = (bf16[2,16,32,256]{3,1,2,0:T(8,128)(2,1)}, bf16[2,16,32,256]{3,1,2,0:T(8,128)(2,1)}, u32[]{:S(2)}, u32[]{:S(2)}) collective-permute-start(bf16[2,16,32,256]{3,1,2,0:T(8,128)(2,1)} %pad_maximum_fusion.2), channel_id=1, source_target_pairs={{128,0},{136,8},{144,16},{152,24},{160,32},{168,40},{176,48},{184,... | collective-permute-start | bytes 1572872 | tf_op jit(solution)/shard_map/ppermute | solution.py:32
  31.9 2.2 copy-start.15
  31.9 2.6 %copy-start.11 = (pred[16]{0:T(512)(128)(4,1)S(1)}, pred[16]{0:T(512)(128)(4,1)}, u32[]{:S(2)}) copy-start(pred[16]{0:T(512)(128)(4,1)} %get-tuple-element.66) | copy-start | bytes 52
  31.9 2.6 %copy-start.12 = (pred[16]{0:T(512)(128)(4,1)S(1)}, pred[16]{0:T(512)(128)(4,1)}, u32[]{:S(2)}) copy-start(pred[16]{0:T(512)(128)(4,1)} %get-tuple-element.67) | copy-start | bytes 52
  31.9 2.6 %copy-start.13 = (pred[16]{0:T(512)(128)(4,1)S(1)}, pred[16]{0:T(512)(128)(4,1)}, u32[]{:S(2)}) copy-start(pred[16]{0:T(512)(128)(4,1)} %get-tuple-element.68) | copy-start | bytes 52
  31.9 2.6 %copy-start.14 = (pred[16]{0:T(512)(128)(4,1)S(1)}, pred[16]{0:T(512)(128)(4,1)}, u32[]{:S(2)}) copy-start(pred[16]{0:T(512)(128)(4,1)} %get-tuple-element.69) | copy-start | bytes 52
  34.2 11.7 %collective-permute-start.2 = (bf16[2,16,32,256]{3,1,2,0:T(8,128)(2,1)}, bf16[2,16,32,256]{3,1,2,0:T(8,128)(2,1)S(1)}, u32[]{:S(2)}, u32[]{:S(2)}) collective-permute-start(bf16[2,16,32,256]{3,1,2,0:T(8,128)(2,1)} %pad_maximum_fusion.2), channel_id=1, source_target_pairs={{192,0},{200,8},{208,16},{216,24},{224,32},{232,40},{240,48},{248,... | collective-permute-start | bytes 1572872 | tf_op jit(solution)/shard_map/ppermute | solution.py:32
  47.5 1.2 copy-start.5
  47.5 1.8 copy-start.4
  50.1 81.4 %copy-start.1 = (bf16[3,16,4096]{2,1,0:T(8,128)(2,1)S(1)}, bf16[3,16,4096]{2,1,0:T(8,128)(2,1)}, u32[]{:S(2)}) copy-start(bf16[3,16,4096]{2,1,0:T(8,128)(2,1)} %param.18) | copy-start | bytes 1179652
  50.2 82.7 %copy-start.8 = (f32[4096]{0:T(1024)S(1)}, f32[4096]{0:T(1024)}, u32[]{:S(2)}) copy-start(f32[4096]{0:T(1024)} %param.26) | copy-start | bytes 49156
  51.5 113.2 %all-gather.5.cloned.1.call-start = ((), (), s32[]{:S(2)}) async-start(), calls=%async_computation.2 | async-start | bytes 4325376 | tf_op jit(solution)/shard_map/all_gather | solution.py:80
  52.1 133.9 %all-gather.3.cloned.1.call-start = ((), (), s32[]{:S(2)}) async-start(), calls=%async_computation.1 | async-start | bytes 7077888 | tf_op jit(solution)/shard_map/all_gather | solution.py:81
  131.6 2.6 %copy-start.3 = (bf16[4096,256]{1,0:T(8,128)(2,1)S(1)}, bf16[4096,256]{1,0:T(8,128)(2,1)}, u32[]{:S(2)}) copy-start(bf16[4096,256]{1,0:T(8,128)(2,1)} %param.27) | copy-start | bytes 6291460
  134.7 25.9 %collective-permute-start.9 = (bf16[3,4,256]{2,1,0:T(4,128)(2,1)S(1)}, bf16[3,4,256]{2,1,0:T(4,128)(2,1)S(1)}, u32[]{:S(2)}, u32[]{:S(2)}) collective-permute-start(bf16[3,4,256]{2,1,0:T(4,128)(2,1)S(1)} %get-tuple-element.43), channel_id=1, source_target_pairs={{0,24},{8,56},{16,88},{24,120},{32,152},{40,184},{48,216},{56,248}... | collective-permute-start | bytes 18440 | tf_op jit(solution)/shard_map/ppermute | solution.py:166
  139.3 21.3 %collective-permute-start.8 = (bf16[3,4,256]{2,1,0:T(4,128)(2,1)S(1)}, bf16[3,4,256]{2,1,0:T(4,128)(2,1)S(1)}, u32[]{:S(2)}, u32[]{:S(2)}) collective-permute-start(bf16[3,4,256]{2,1,0:T(4,128)(2,1)S(1)} %get-tuple-element.44), channel_id=1, source_target_pairs={{0,16},{8,48},{16,80},{24,112},{32,144},{40,176},{48,208},{56,240}... | collective-permute-start | bytes 18440 | tf_op jit(solution)/shard_map/ppermute | solution.py:166
  151.8 8.8 %collective-permute-start.7 = (bf16[3,4,256]{2,1,0:T(4,128)(2,1)S(1)}, bf16[3,4,256]{2,1,0:T(4,128)(2,1)S(1)}, u32[]{:S(2)}, u32[]{:S(2)}) collective-permute-start(bf16[3,4,256]{2,1,0:T(4,128)(2,1)S(1)} %get-tuple-element.45), channel_id=1, source_target_pairs={{0,8},{8,40},{16,72},{24,104},{32,136},{40,168},{48,200},{56,232},... | collective-permute-start | bytes 18440 | tf_op jit(solution)/shard_map/ppermute | solution.py:166
  157.3 7.4 %collective-permute-start.6 = (bf16[3,4,256]{2,1,0:T(4,128)(2,1)S(1)}, bf16[3,4,256]{2,1,0:T(4,128)(2,1)S(1)}, u32[]{:S(2)}, u32[]{:S(2)}) collective-permute-start(bf16[3,4,256]{2,1,0:T(4,128)(2,1)S(1)} %get-tuple-element.42), channel_id=1, source_target_pairs={{0,0},{8,32},{16,64},{24,96},{32,128},{40,160},{48,192},{56,224},{... | collective-permute-start | bytes 18440 | tf_op jit(solution)/shard_map/ppermute | solution.py:166
  194.3 16.3 %collective-permute-start.13 = (bf16[3,4,256]{2,1,0:T(4,128)(2,1)S(1)}, bf16[3,4,256]{2,1,0:T(4,128)(2,1)S(1)}, u32[]{:S(2)}, u32[]{:S(2)}) collective-permute-start(bf16[3,4,256]{2,1,0:T(4,128)(2,1)S(1)} %squeeze.124), channel_id=1, source_target_pairs={{24,0},{56,8},{88,16},{120,24},{152,32},{184,40},{216,48},{248,56}... | collective-permute-start | bytes 18440 | tf_op jit(solution)/shard_map/ppermute | solution.py:177
  199.9 10.7 %collective-permute-start.12 = (bf16[3,4,256]{2,1,0:T(4,128)(2,1)S(1)}, bf16[3,4,256]{2,1,0:T(4,128)(2,1)S(1)}, u32[]{:S(2)}, u32[]{:S(2)}) collective-permute-start(bf16[3,4,256]{2,1,0:T(4,128)(2,1)S(1)} %squeeze.123), channel_id=1, source_target_pairs={{16,0},{48,8},{80,16},{112,24},{144,32},{176,40},{208,48},{240,56}... | collective-permute-start | bytes 18440 | tf_op jit(solution)/shard_map/ppermute | solution.py:177
  201.7 8.9 %collective-permute-start.11 = (bf16[3,4,256]{2,1,0:T(4,128)(2,1)S(1)}, bf16[3,4,256]{2,1,0:T(4,128)(2,1)S(1)}, u32[]{:S(2)}, u32[]{:S(2)}) collective-permute-start(bf16[3,4,256]{2,1,0:T(4,128)(2,1)S(1)} %squeeze.122), channel_id=1, source_target_pairs={{8,0},{40,8},{72,16},{104,24},{136,32},{168,40},{200,48},{232,56},... | collective-permute-start | bytes 18440 | tf_op jit(solution)/shard_map/ppermute | solution.py:177
  207.6 8.6 %collective-permute-start.10 = (bf16[3,4,256]{2,1,0:T(4,128)(2,1)S(1)}, bf16[3,4,256]{2,1,0:T(4,128)(2,1)S(1)}, u32[]{:S(2)}, u32[]{:S(2)}) collective-permute-start(bf16[3,4,256]{2,1,0:T(4,128)(2,1)S(1)} %squeeze.121), channel_id=1, source_target_pairs={{0,0},{32,8},{64,16},{96,24},{128,32},{160,40},{192,48},{224,56},{... | collective-permute-start | bytes 18440 | tf_op jit(solution)/shard_map/ppermute | solution.py:177
  (1 other events, 0.5 us)
Sparse Core Ops, SparseCore 0:
  51.6 79.8 all-reduce.1
Sparse Core Ops, SparseCore 1:
  54.5 55.5 all-gather.4
  111.8 74.1 all-gather.2
where the time goes:
time: 225 us
  waiting for transfers between devices  121 us (54%)
  starting transfers between devices  48.4 us (22%)
  between operations  16.9 us (8%)
  matrix products  16.7 us (7%)
  other arithmetic  13.6 us (6%)
  local copies, waits for them, and re-layouts  8.23 us (4%)
    psum x1, waiting for transfers between devices, shards(): lax.psum(partial_out.astype(jnp.bfloat16), 'head').astype(jnp.float32)  78.1 us
    ppermute x4, starting transfers between devices, shards(): sent.append(lax.ppermute(piece, 'hyp', route))  25.9 us
    all_gather x1, waiting for transfers between devices, shards(): full_rows = lax.all_gather(encoder_rows, 'head', axis=1, tiled=True)  21.2 us
    ppermute x4, starting transfers between devices, shards(): back.append(lax.ppermute(answer[shift], 'hyp', route))  16.2 us
    ppermute x6, waiting for transfers between devices, beam_copies(): copies.append(lax.ppermute(block, 'hyp', route))  11.1 us
    dot_general x1, matrix products, shards(): jnp.dot(full_rows, full_weights, preferred_element_type=jnp.float32)  7.47 us
    ppermute x6, starting transfers between devices, beam_copies(): copies.append(lax.ppermute(block, 'hyp', route))  6.19 us
    ppermute x4, waiting for transfers between devices, shards(): back.append(lax.ppermute(answer[shift], 'hyp', route))  5.57 us
  transfers between devices with their start and end apart: 17, of which 5 were waited for; matrix products, arithmetic and copies ran while one was open for 7% of the time, Pallas kernels for 0%

commit v1 on v0

--- a/solution.py
+++ b/solution.py
@@ -78,7 +78,9 @@
     past_len = past_keys.shape[1]
     scaling = HEAD ** (-0.5)
     full_weights = lax.all_gather(cross_wkv, "hyp", axis=0, tiled=True)
-    full_rows = lax.all_gather(encoder_rows, "head", axis=1, tiled=True)
+    full_rows = jnp.concatenate(
+        lax.all_to_all(jnp.stack([encoder_rows] * lax.axis_size("head")), "head", 0, 0), axis=1
+    )
     cross_kv = jnp.dot(full_rows, full_weights, preferred_element_type=jnp.float32).astype(
         jnp.bfloat16
     )

time: 225 us -> 241 us (1.071)
  starting transfers between devices: 48.4 us -> 73.9 us
  waiting for transfers between devices: 121 us -> 108 us
  local copies, waits for them, and re-layouts: 8.23 us -> 11.7 us
    all_gather x1 -> x0, waiting for transfers between devices: 21.2 us -> none  [shards(): full_rows = lax.all_gather(encoder_rows, 'head', axis=1, tiled=True)]
    ppermute x4, starting transfers between devices: 25.9 us -> 46 us  [shards(): sent.append(lax.ppermute(piece, 'hyp', route))]
    psum x1, waiting for transfers between devices: 78.1 us -> 89.3 us  [shards(): lax.psum(partial_out.astype(jnp.bfloat16), 'head').astype(jnp.float32)]
    all_to_all x0 -> x1, starting transfers between devices: none -> 8.32 us  [shards(): lax.all_to_all(jnp.stack([encoder_rows] * lax.axis_size('head')), 'head',...]
    eq x10, other arithmetic: 3.41 us -> 0.12 us  [pick_rows(): selector == position]
    another operation x0 -> x1, local copies, waits for them, and re-layouts: none -> 3.04 us  [shards(): jnp.stack([encoder_rows] * lax.axis_size('head'))]
    ppermute x4, starting transfers between devices: 16.2 us -> 13.2 us  [shards(): back.append(lax.ppermute(answer[shift], 'hyp', route))]
  transfers between devices with their start and end apart: 17 -> 17, of which waited for: 5 -> 4; matrix products, arithmetic and copies ran while one was open for 7% -> 9% of each run, Pallas kernels for 0% -> 0%
where the time goes in v1:
time: 241 us; the launch traced here: 239 us
  waiting for transfers between devices  108 us (45%)
  starting transfers between devices  73.9 us (31%)
  between operations  16.9 us (7%)
  matrix products  16.7 us (7%)
  other arithmetic  11.9 us (5%)
  local copies, waits for them, and re-layouts  11.7 us (5%)
    psum x1, waiting for transfers between devices, shards(): lax.psum(partial_out.astype(jnp.bfloat16), 'head').astype(jnp.float32)  89.3 us
    ppermute x4, starting transfers between devices, shards(): sent.append(lax.ppermute(piece, 'hyp', route))  46 us
    ppermute x4, starting transfers between devices, shards(): back.append(lax.ppermute(answer[shift], 'hyp', route))  13.2 us
    ppermute x6, waiting for transfers between devices, beam_copies(): copies.append(lax.ppermute(block, 'hyp', route))  9.42 us
    all_to_all x1, starting transfers between devices, shards(): lax.all_to_all(jnp.stack([encoder_rows] * lax.axis_size('head')), 'head',...  8.32 us
    dot_general x1, matrix products, shards(): jnp.dot(full_rows, full_weights, preferred_element_type=jnp.float32)  7.47 us
    ppermute x6, starting transfers between devices, beam_copies(): copies.append(lax.ppermute(block, 'hyp', route))  6.22 us
    ppermute x4, waiting for transfers between devices, shards(): back.append(lax.ppermute(answer[shift], 'hyp', route))  4.83 us
  transfers between devices with their start and end apart: 17, of which 4 were waited for; matrix products, arithmetic and copies ran while one was open for 9% of the time, Pallas kernels for 0%

profile of v1, /device:TPU:17, one launch (start us, length us, event | category | flops | bytes accessed | tf_op | source)
XLA Modules:
  0.0 239.2 jit_solution(6611355574590929312)
XLA Ops:
  8.0 0.9 constant_dynamic-slice_fusion
  9.1 1.1 fusion.42
  10.2 1.3 multiply_reduce_fusion.1
  11.5 1.2 multiply_convert_fusion.1
  12.7 2.1 convolution_convert_fusion.4
  16.1 2.6 %collective-permute-start.4 = (bf16[2,3,16,256]{3,2,0,1:T(8,128)(2,1)}, bf16[2,3,16,256]{3,2,0,1:T(8,128)(2,1)}, u32[]{:S(2)}, u32[]{:S(2)}) collective-permute-start(bf16[2,3,16,256]{3,2,0,1:T(8,128)(2,1)} %pad_maximum_fusion.4), channel_id=1, source_target_pairs={{128,0},{136,8},{144,16},{152,24},{160,32},{168,40},{176,48},{184,... | collective-permute-start | bytes 147464 | tf_op jit(solution)/shard_map/ppermute | solution.py:32
  19.1 1.0 pad_maximum_fusion.2
  20.1 1.5 collective-permute-start
  21.5 1.6 collective-permute-start.1
  23.2 1.4 copy.52
  24.6 3.0 %stack.86 = bf16[8,768,512]{1,2,0:T(8,128)(2,1)} broadcast(bf16[768,512]{0,1:T(8,128)(2,1)S(1)} %copy.52), dimensions={1,2} | broadcast | bytes 7077888 | tf_op jit(solution)/shard_map/stack | solution.py:82
  27.6 8.3 %all-to-all-start = ((bf16[8,768,512]{1,2,0:T(8,128)(2,1)}), bf16[8,768,512]{1,2,0:T(8,128)(2,1)}, u32[]{:S(2)}, u32[]{:S(2)}) async-start(bf16[8,768,512]{1,2,0:T(8,128)(2,1)} %stack.86), calls=%async_computation | async-start | bytes 12582912 | tf_op jit(solution)/shard_map/all_to_all | solution.py:82
  40.7 2.1 convolution_convert_fusion.6
  43.2 0.9 fusion.35
  44.1 0.8 fusion.32
  44.9 9.4 %collective-permute-done.2 = bf16[2,16,32,256]{3,1,2,0:T(8,128)(2,1)S(1)} collective-permute-done((bf16[2,16,32,256]{3,1,2,0:T(8,128)(2,1)}, bf16[2,16,32,256]{3,1,2,0:T(8,128)(2,1)S(1)}, u32[]{:S(2)}, u32[]{:S(2)}) %collective-permute-start.2) | collective-permute-done | bytes 524320 | tf_op jit(solution)/shard_map/ppermute | solution.py:32
  54.3 1.5 select_select_fusion.2
  58.7 1.2 convolution_convert_fusion
  61.3 89.3 %all-reduce.2.cloned.1.call-done = bf16[3,16,4096]{2,1,0:T(8,128)(2,1)} async-done(((bf16[3,16,4096]{2,1,0:T(8,128)(2,1)}), bf16[3,16,4096]{2,1,0:T(8,128)(2,1)}) %all-reduce.2.cloned.1.call-update) | async-done | bytes 393232 | tf_op jit(solution)/shard_map/psum | solution.py:153
  150.6 1.4 multiply_reduce_fusion
  152.0 1.2 multiply_convert_fusion
  153.7 5.6 %collective-permute-start.9 = (bf16[3,4,256]{2,1,0:T(4,128)(2,1)S(1)}, bf16[3,4,256]{2,1,0:T(4,128)(2,1)S(1)}, u32[]{:S(2)}, u32[]{:S(2)}) collective-permute-start(bf16[3,4,256]{2,1,0:T(4,128)(2,1)S(1)} %get-tuple-element.43), channel_id=1, source_target_pairs={{0,24},{8,56},{16,88},{24,120},{32,152},{40,184},{48,216},{56,248}... | collective-permute-start | bytes 18440 | tf_op jit(solution)/shard_map/ppermute | solution.py:168
  159.3 2.6 %collective-permute-start.8 = (bf16[3,4,256]{2,1,0:T(4,128)(2,1)S(1)}, bf16[3,4,256]{2,1,0:T(4,128)(2,1)S(1)}, u32[]{:S(2)}, u32[]{:S(2)}) collective-permute-start(bf16[3,4,256]{2,1,0:T(4,128)(2,1)S(1)} %get-tuple-element.44), channel_id=1, source_target_pairs={{0,16},{8,48},{16,80},{24,112},{32,144},{40,176},{48,208},{56,240}... | collective-permute-start | bytes 18440 | tf_op jit(solution)/shard_map/ppermute | solution.py:168
  162.0 34.5 %collective-permute-start.7 = (bf16[3,4,256]{2,1,0:T(4,128)(2,1)S(1)}, bf16[3,4,256]{2,1,0:T(4,128)(2,1)S(1)}, u32[]{:S(2)}, u32[]{:S(2)}) collective-permute-start(bf16[3,4,256]{2,1,0:T(4,128)(2,1)S(1)} %get-tuple-element.45), channel_id=1, source_target_pairs={{0,8},{8,40},{16,72},{24,104},{32,136},{40,168},{48,200},{56,232},... | collective-permute-start | bytes 18440 | tf_op jit(solution)/shard_map/ppermute | solution.py:168
  196.5 3.3 %collective-permute-start.6 = (bf16[3,4,256]{2,1,0:T(4,128)(2,1)S(1)}, bf16[3,4,256]{2,1,0:T(4,128)(2,1)S(1)}, u32[]{:S(2)}, u32[]{:S(2)}) collective-permute-start(bf16[3,4,256]{2,1,0:T(4,128)(2,1)S(1)} %get-tuple-element.42), channel_id=1, source_target_pairs={{0,0},{8,32},{16,64},{24,96},{32,128},{40,160},{48,192},{56,224},{... | collective-permute-start | bytes 18440 | tf_op jit(solution)/shard_map/ppermute | solution.py:168
  199.8 4.0 %collective-permute-done.6 = bf16[3,4,256]{2,1,0:T(4,128)(2,1)S(1)} collective-permute-done((bf16[3,4,256]{2,1,0:T(4,128)(2,1)S(1)}, bf16[3,4,256]{2,1,0:T(4,128)(2,1)S(1)}, u32[]{:S(2)}, u32[]{:S(2)}) %collective-permute-start.6) | collective-permute-done | bytes 6176 | tf_op jit(solution)/shard_map/ppermute | solution.py:168
  203.9 7.5 %convolution_convert_fusion.1 = bf16[768,512]{0,1:T(8,128)(2,1)S(1)} fusion(bf16[768,4096]{0,1:T(8,128)(2,1)} %bitcast.91, bf16[4096,512]{1,0:T(8,128)(2,1)} %all-gather.2.cloned.1.call-done), kind=kOutput, calls=%fused_computation.8 | convolution fusion | flops 3221618688 | bytes 11272192 | tf_op jit(solution)/shard_map/dot_general | solution.py:84
  212.3 1.9 collective-permute-start.13
  214.2 3.4 %collective-permute-start.12 = (bf16[3,4,256]{2,1,0:T(4,128)(2,1)S(1)}, bf16[3,4,256]{2,1,0:T(4,128)(2,1)S(1)}, u32[]{:S(2)}, u32[]{:S(2)}) collective-permute-start(bf16[3,4,256]{2,1,0:T(4,128)(2,1)S(1)} %squeeze.123), channel_id=1, source_target_pairs={{16,0},{48,8},{80,16},{112,24},{144,32},{176,40},{208,48},{240,56}... | collective-permute-start | bytes 18440 | tf_op jit(solution)/shard_map/ppermute | solution.py:179
  217.6 4.2 %collective-permute-start.11 = (bf16[3,4,256]{2,1,0:T(4,128)(2,1)S(1)}, bf16[3,4,256]{2,1,0:T(4,128)(2,1)S(1)}, u32[]{:S(2)}, u32[]{:S(2)}) collective-permute-start(bf16[3,4,256]{2,1,0:T(4,128)(2,1)S(1)} %squeeze.122), channel_id=1, source_target_pairs={{8,0},{40,8},{72,16},{104,24},{136,32},{168,40},{200,48},{232,56},... | collective-permute-start | bytes 18440 | tf_op jit(solution)/shard_map/ppermute | solution.py:179
  221.9 3.7 %collective-permute-start.10 = (bf16[3,4,256]{2,1,0:T(4,128)(2,1)S(1)}, bf16[3,4,256]{2,1,0:T(4,128)(2,1)S(1)}, u32[]{:S(2)}, u32[]{:S(2)}) collective-permute-start(bf16[3,4,256]{2,1,0:T(4,128)(2,1)S(1)} %squeeze.121), channel_id=1, source_target_pairs={{0,0},{32,8},{64,16},{96,24},{128,32},{160,40},{192,48},{224,56},{... | collective-permute-start | bytes 18440 | tf_op jit(solution)/shard_map/ppermute | solution.py:179
  225.6 4.8 %collective-permute-done.10 = bf16[3,4,256]{2,1,0:T(4,128)(2,1)S(1)} collective-permute-done((bf16[3,4,256]{2,1,0:T(4,128)(2,1)S(1)}, bf16[3,4,256]{2,1,0:T(4,128)(2,1)S(1)}, u32[]{:S(2)}, u32[]{:S(2)}) %collective-permute-start.10) | collective-permute-done | bytes 6176 | tf_op jit(solution)/shard_map/ppermute | solution.py:179
  (137 shorter events, 12.9 us)
Async XLA Ops:
  8.0 50.7 %copy-start = (bf16[256,4096]{1,0:T(8,128)(2,1)S(1)}, bf16[256,4096]{1,0:T(8,128)(2,1)}, u32[]{:S(2)}) copy-start(bf16[256,4096]{1,0:T(8,128)(2,1)} %param.25) | copy-start | bytes 6291460
  10.2 4.7 %copy-start.6 = (bf16[4096,256]{1,0:T(8,128)(2,1)S(1)}, bf16[4096,256]{1,0:T(8,128)(2,1)}, u32[]{:S(2)}) copy-start(bf16[4096,256]{1,0:T(8,128)(2,1)} %param.23) | copy-start | bytes 6291460
  12.7 6.1 %copy-start.14 = (bf16[16,32,256]{2,1,0:T(8,128)(2,1)S(1)}, bf16[16,32,256]{2,1,0:T(8,128)(2,1)}, u32[]{:S(2)}) copy-start(bf16[16,32,256]{2,1,0:T(8,128)(2,1)} %param.32) | copy-start | bytes 786436
  12.7 6.1 %copy-start.15 = (bf16[16,32,256]{2,1,0:T(8,128)(2,1)S(1)}, bf16[16,32,256]{2,1,0:T(8,128)(2,1)}, u32[]{:S(2)}) copy-start(bf16[16,32,256]{2,1,0:T(8,128)(2,1)} %param.31) | copy-start | bytes 786436
  14.8 5.2 %copy-start.9 = (bf16[48,256]{1,0:T(8,128)(2,1)}, bf16[48,256]{1,0:T(8,128)(2,1)S(1)}, u32[]{:S(2)}) copy-start(bf16[48,256]{1,0:T(8,128)(2,1)S(1)} %convolution_convert_fusion.4) | copy-start | bytes 73732
  15.3 6.2 %copy-start.11 = (bf16[48,256]{1,0:T(8,128)(2,1)}, bf16[48,256]{1,0:T(8,128)(2,1)S(1)}, u32[]{:S(2)}) copy-start(bf16[48,256]{1,0:T(8,128)(2,1)S(1)} %convolution_convert_fusion.5) | copy-start | bytes 73732
  16.0 26.8 %collective-permute-start.3 = (bf16[2,3,16,256]{3,2,0,1:T(8,128)(2,1)}, bf16[2,3,16,256]{3,2,0,1:T(8,128)(2,1)}, u32[]{:S(2)}, u32[]{:S(2)}) collective-permute-start(bf16[2,3,16,256]{3,2,0,1:T(8,128)(2,1)} %pad_maximum_fusion.4), channel_id=1, source_target_pairs={{64,0},{72,8},{80,16},{88,24},{96,32},{104,40},{112,48},{120,56},{... | collective-permute-start | bytes 147464 | tf_op jit(solution)/shard_map/ppermute | solution.py:32
  16.1 27.0 %collective-permute-start.4 = (bf16[2,3,16,256]{3,2,0,1:T(8,128)(2,1)}, bf16[2,3,16,256]{3,2,0,1:T(8,128)(2,1)}, u32[]{:S(2)}, u32[]{:S(2)}) collective-permute-start(bf16[2,3,16,256]{3,2,0,1:T(8,128)(2,1)} %pad_maximum_fusion.4), channel_id=1, source_target_pairs={{128,0},{136,8},{144,16},{152,24},{160,32},{168,40},{176,48},{184,... | collective-permute-start | bytes 147464 | tf_op jit(solution)/shard_map/ppermute | solution.py:32
  18.8 24.4 %collective-permute-start.5 = (bf16[2,3,16,256]{3,2,0,1:T(8,128)(2,1)}, bf16[2,3,16,256]{3,2,0,1:T(8,128)(2,1)}, u32[]{:S(2)}, u32[]{:S(2)}) collective-permute-start(bf16[2,3,16,256]{3,2,0,1:T(8,128)(2,1)} %pad_maximum_fusion.4), channel_id=1, source_target_pairs={{192,0},{200,8},{208,16},{216,24},{224,32},{232,40},{240,48},{248,... | collective-permute-start | bytes 147464 | tf_op jit(solution)/shard_map/ppermute | solution.py:32
  19.1 2.5 %copy-start.2 = (bf16[1,16,32,256]{3,1,2,0:T(8,128)(2,1)}, bf16[1,16,32,256]{3,1,2,0:T(8,128)(2,1)S(1)}, u32[]{:S(2)}) copy-start(bf16[1,16,32,256]{3,1,2,0:T(8,128)(2,1)S(1)} %get-tuple-element.74) | copy-start | bytes 786436
  20.1 24.8 %collective-permute-start = (bf16[2,16,32,256]{3,1,2,0:T(8,128)(2,1)}, bf16[2,16,32,256]{3,1,2,0:T(8,128)(2,1)}, u32[]{:S(2)}, u32[]{:S(2)}) collective-permute-start(bf16[2,16,32,256]{3,1,2,0:T(8,128)(2,1)} %pad_maximum_fusion.2), channel_id=1, source_target_pairs={{64,0},{72,8},{80,16},{88,24},{96,32},{104,40},{112,48},{120,56},{... | collective-permute-start | bytes 1572872 | tf_op jit(solution)/shard_map/ppermute | solution.py:32
  21.5 23.4 %collective-permute-start.1 = (bf16[2,16,32,256]{3,1,2,0:T(8,128)(2,1)}, bf16[2,16,32,256]{3,1,2,0:T(8,128)(2,1)}, u32[]{:S(2)}, u32[]{:S(2)}) collective-permute-start(bf16[2,16,32,256]{3,1,2,0:T(8,128)(2,1)} %pad_maximum_fusion.2), channel_id=1, source_target_pairs={{128,0},{136,8},{144,16},{152,24},{160,32},{168,40},{176,48},{184,... | collective-permute-start | bytes 1572872 | tf_op jit(solution)/shard_map/ppermute | solution.py:32
  27.6 8.4 %copy-start.17 = (s32[3,512]{1,0:T(4,128)S(1)}, s32[3,512]{1,0:T(4,128)}, u32[]{:S(2)}) copy-start(s32[3,512]{1,0:T(4,128)} %param.33) | copy-start | bytes 18436
  27.6 176.3 %all-to-all-start = ((bf16[8,768,512]{1,2,0:T(8,128)(2,1)}), bf16[8,768,512]{1,2,0:T(8,128)(2,1)}, u32[]{:S(2)}, u32[]{:S(2)}) async-start(bf16[8,768,512]{1,2,0:T(8,128)(2,1)} %stack.86), calls=%async_computation | async-start | bytes 12582912 | tf_op jit(solution)/shard_map/all_to_all | solution.py:82
  35.9 114.7 %all-reduce.2.cloned.1.call-start = ((), (), s32[]{:S(2)}) async-start(), calls=%async_computation.1 | async-start | bytes 786432 | tf_op jit(solution)/shard_map/psum | solution.py:153
  38.4 4.7 %copy-start.10 = (bf16[48,256]{1,0:T(8,128)(2,1)S(1)}, bf16[48,256]{1,0:T(8,128)(2,1)}, u32[]{:S(2)}) copy-start(bf16[48,256]{1,0:T(8,128)(2,1)} %copy-done.9) | copy-start | bytes 73732
  38.5 4.7 %copy-start.12 = (bf16[48,256]{1,0:T(8,128)(2,1)S(1)}, bf16[48,256]{1,0:T(8,128)(2,1)}, u32[]{:S(2)}) copy-start(bf16[48,256]{1,0:T(8,128)(2,1)} %copy-done.11) | copy-start | bytes 73732
  39.1 15.2 %copy-start.3 = (bf16[1,16,32,256]{3,1,2,0:T(8,128)(2,1)S(1)}, bf16[1,16,32,256]{3,1,2,0:T(8,128)(2,1)}, u32[]{:S(2)}) copy-start(bf16[1,16,32,256]{3,1,2,0:T(8,128)(2,1)} %copy-done.2) | copy-start | bytes 786436
  39.1 15.2 %copy-start.5 = (bf16[1,16,32,256]{3,1,2,0:T(8,128)(2,1)S(1)}, bf16[1,16,32,256]{3,1,2,0:T(8,128)(2,1)}, u32[]{:S(2)}) copy-start(bf16[1,16,32,256]{3,1,2,0:T(8,128)(2,1)} %copy-done.4) | copy-start | bytes 786436
  42.8 11.5 %collective-permute-start.2 = (bf16[2,16,32,256]{3,1,2,0:T(8,128)(2,1)}, bf16[2,16,32,256]{3,1,2,0:T(8,128)(2,1)S(1)}, u32[]{:S(2)}, u32[]{:S(2)}) collective-permute-start(bf16[2,16,32,256]{3,1,2,0:T(8,128)(2,1)} %pad_maximum_fusion.2), channel_id=1, source_target_pairs={{192,0},{200,8},{208,16},{216,24},{224,32},{232,40},{240,48},{248,... | collective-permute-start | bytes 1572872 | tf_op jit(solution)/shard_map/ppermute | solution.py:32
  57.7 92.9 %copy-start.1 = (bf16[3,16,4096]{2,1,0:T(8,128)(2,1)S(1)}, bf16[3,16,4096]{2,1,0:T(8,128)(2,1)}, u32[]{:S(2)}) copy-start(bf16[3,16,4096]{2,1,0:T(8,128)(2,1)} %param.18) | copy-start | bytes 1179652
  58.7 93.3 %copy-start.16 = (f32[4096]{0:T(1024)S(1)}, f32[4096]{0:T(1024)}, u32[]{:S(2)}) copy-start(f32[4096]{0:T(1024)} %param.26) | copy-start | bytes 49156
  60.0 143.9 %all-gather.2.cloned.1.call-start = ((), (), s32[]{:S(2)}) async-start(), calls=%async_computation.2 | async-start | bytes 4325376 | tf_op jit(solution)/shard_map/all_gather | solution.py:80
  150.6 2.6 %copy-start.7 = (bf16[4096,256]{1,0:T(8,128)(2,1)S(1)}, bf16[4096,256]{1,0:T(8,128)(2,1)}, u32[]{:S(2)}) copy-start(bf16[4096,256]{1,0:T(8,128)(2,1)} %param.27) | copy-start | bytes 6291460
  153.7 46.1 %collective-permute-start.9 = (bf16[3,4,256]{2,1,0:T(4,128)(2,1)S(1)}, bf16[3,4,256]{2,1,0:T(4,128)(2,1)S(1)}, u32[]{:S(2)}, u32[]{:S(2)}) collective-permute-start(bf16[3,4,256]{2,1,0:T(4,128)(2,1)S(1)} %get-tuple-element.43), channel_id=1, source_target_pairs={{0,24},{8,56},{16,88},{24,120},{32,152},{40,184},{48,216},{56,248}... | collective-permute-start | bytes 18440 | tf_op jit(solution)/shard_map/ppermute | solution.py:168
  159.3 40.5 %collective-permute-start.8 = (bf16[3,4,256]{2,1,0:T(4,128)(2,1)S(1)}, bf16[3,4,256]{2,1,0:T(4,128)(2,1)S(1)}, u32[]{:S(2)}, u32[]{:S(2)}) collective-permute-start(bf16[3,4,256]{2,1,0:T(4,128)(2,1)S(1)} %get-tuple-element.44), channel_id=1, source_target_pairs={{0,16},{8,48},{16,80},{24,112},{32,144},{40,176},{48,208},{56,240}... | collective-permute-start | bytes 18440 | tf_op jit(solution)/shard_map/ppermute | solution.py:168
  162.0 37.9 %collective-permute-start.7 = (bf16[3,4,256]{2,1,0:T(4,128)(2,1)S(1)}, bf16[3,4,256]{2,1,0:T(4,128)(2,1)S(1)}, u32[]{:S(2)}, u32[]{:S(2)}) collective-permute-start(bf16[3,4,256]{2,1,0:T(4,128)(2,1)S(1)} %get-tuple-element.45), channel_id=1, source_target_pairs={{0,8},{8,40},{16,72},{24,104},{32,136},{40,168},{48,200},{56,232},... | collective-permute-start | bytes 18440 | tf_op jit(solution)/shard_map/ppermute | solution.py:168
  196.5 7.4 %collective-permute-start.6 = (bf16[3,4,256]{2,1,0:T(4,128)(2,1)S(1)}, bf16[3,4,256]{2,1,0:T(4,128)(2,1)S(1)}, u32[]{:S(2)}, u32[]{:S(2)}) collective-permute-start(bf16[3,4,256]{2,1,0:T(4,128)(2,1)S(1)} %get-tuple-element.42), channel_id=1, source_target_pairs={{0,0},{8,32},{16,64},{24,96},{32,128},{40,160},{48,192},{56,224},{... | collective-permute-start | bytes 18440 | tf_op jit(solution)/shard_map/ppermute | solution.py:168
  212.3 13.3 %collective-permute-start.13 = (bf16[3,4,256]{2,1,0:T(4,128)(2,1)S(1)}, bf16[3,4,256]{2,1,0:T(4,128)(2,1)S(1)}, u32[]{:S(2)}, u32[]{:S(2)}) collective-permute-start(bf16[3,4,256]{2,1,0:T(4,128)(2,1)S(1)} %squeeze.124), channel_id=1, source_target_pairs={{24,0},{56,8},{88,16},{120,24},{152,32},{184,40},{216,48},{248,56}... | collective-permute-start | bytes 18440 | tf_op jit(solution)/shard_map/ppermute | solution.py:179
  214.2 11.4 %collective-permute-start.12 = (bf16[3,4,256]{2,1,0:T(4,128)(2,1)S(1)}, bf16[3,4,256]{2,1,0:T(4,128)(2,1)S(1)}, u32[]{:S(2)}, u32[]{:S(2)}) collective-permute-start(bf16[3,4,256]{2,1,0:T(4,128)(2,1)S(1)} %squeeze.123), channel_id=1, source_target_pairs={{16,0},{48,8},{80,16},{112,24},{144,32},{176,40},{208,48},{240,56}... | collective-permute-start | bytes 18440 | tf_op jit(solution)/shard_map/ppermute | solution.py:179
  217.6 8.0 %collective-permute-start.11 = (bf16[3,4,256]{2,1,0:T(4,128)(2,1)S(1)}, bf16[3,4,256]{2,1,0:T(4,128)(2,1)S(1)}, u32[]{:S(2)}, u32[]{:S(2)}) collective-permute-start(bf16[3,4,256]{2,1,0:T(4,128)(2,1)S(1)} %squeeze.122), channel_id=1, source_target_pairs={{8,0},{40,8},{72,16},{104,24},{136,32},{168,40},{200,48},{232,56},... | collective-permute-start | bytes 18440 | tf_op jit(solution)/shard_map/ppermute | solution.py:179
  221.9 8.6 %collective-permute-start.10 = (bf16[3,4,256]{2,1,0:T(4,128)(2,1)S(1)}, bf16[3,4,256]{2,1,0:T(4,128)(2,1)S(1)}, u32[]{:S(2)}, u32[]{:S(2)}) collective-permute-start(bf16[3,4,256]{2,1,0:T(4,128)(2,1)S(1)} %squeeze.121), channel_id=1, source_target_pairs={{0,0},{32,8},{64,16},{96,24},{128,32},{160,40},{192,48},{224,56},{... | collective-permute-start | bytes 18440 | tf_op jit(solution)/shard_map/ppermute | solution.py:179
  (3 other events, 5.2 us)
Sparse Core Ops, SparseCore 0:
  60.1 90.4 all-reduce.1
Sparse Core Ops, SparseCore 1:
  63.0 54.0 all-gather.1
